TPU v7x, 32 devices: a whole 2x2x4 slice. The times are simulated.
32 devices in a mesh: groups: 2 (over y), row: 8 (over z, x), col: 2 (over core).
Axes of the slice: x: 2, y: 2, z: 4, core: 2. Of those that a mesh axis runs over, the one named last changes fastest.
Arguments:
- tokens: bfloat16 [4, 1024, 3584], P('groups', 'row', 'col'), parts along dimension 0, may hold values from -40 to 40
- gain: float32 [3584], replicated, may hold values from 0.5 to 2
- w_query: bfloat16 [3584, 1792], P('row', 'col'), may hold values from -0.125 to 0.125
- b_query: float32 [1792], P('col'), may hold values from -24 to 24
- key_weight: bfloat16 [3584, 256], P('row', 'col'), may hold values from -0.125 to 0.125
- b_key: float32 [256], P('col'), may hold values from -24 to 24
- value_weight: bfloat16 [3584, 256], P('row', 'col'), may hold values from -0.09375 to 0.09375
- value_bias: float32 [256], P('col'), may hold values from -3 to 3
- random_block_index: int32 [4, 16, 14, 2], P('groups'), parts along dimension 0, may hold values from 0 to 15, as said below
- global_block_index: int32 [4, 2, 2], P('groups'), parts along dimension 0, may hold values from 0 to 15
Outputs:
- context: bfloat16 [4, 1024, 1792], P('groups', 'row', 'col'), parts along dimension 0
There are 2 independent parts, one for each index of `groups`. A program takes and returns all parts, laid end to end along the dimension named above; an argument that names none is the same for every part. Nothing has to cross between parts.
Inputs may be any that keep to these rules, and one draw needn't show every extreme that they name: `random_block_index`: A request group is the 56 entries of both passages whose query block lies in one aligned run of 2 blocks and whose head lies in one aligned run of 7 heads. In every request group at most 7 entries name blocks of any one aligned run of 2 blocks, and some run is named exactly 7 times.
All inputs are finite; a program needn't handle non-finite values.
Results may differ from a plain program's by a relative error of at most 0.003.
The roundings to bfloat16 on the way count: a program that leaves them out, or rounds other values in their place, can miss the bound.
Values may be sent and summed in bfloat16 or wider, within the bound.
No kernel may reach another device: no remote copies, remote signals or barrier semaphores. Data moves between devices by JAX's collectives and lax.ppermute only.
A program may use at most 128 MiB of HBM per device.

v0:
```python
import math
import jax
import jax.numpy as jnp
from jax import lax
from jax.sharding import PartitionSpec as P

HEAD_SIZE = 128
BLOCK_TOKENS = 64
RANDOM_BLOCKS = 2
GLOBAL_BLOCKS = 2
rope_base = 1000000.0
norm_eps = 1e-06


def broadcast(block, axis, source):
    block = jnp.where(lax.axis_index(axis) == source, block, jnp.zeros_like(block))
    return lax.psum(block, axis)


def padded_2(shard, sides, width):
    for axis, dim in sides:
        count, length = (lax.axis_size(axis), shard.shape[dim])
        up = [(i, (i + 1) % count) for i in range(count - 1)]
        down = [(j, i) for i, j in up]
        last = lax.slice_in_dim(shard, length - width, length, axis=dim)
        leading = lax.slice_in_dim(shard, 0, width, axis=dim)
        before = lax.ppermute(last, axis, up)
        after = lax.ppermute(leading, axis, down)
        shard = jnp.concatenate([before, shard, after], axis=dim)
    return shard


def apply_rotation(values, token_positions):
    half = values.shape[-1] // 2
    freqs = 1.0 / rope_base ** (jnp.arange(half, dtype=jnp.float32) * 2.0 / values.shape[-1])
    angles = token_positions[:, None] * freqs[None, :]
    cosine = jnp.concatenate([jnp.cos(angles), jnp.cos(angles)], axis=-1)[None, :, None, :]
    sine = jnp.concatenate([jnp.sin(angles), jnp.sin(angles)], axis=-1)[None, :, None, :]
    turned = jnp.concatenate([-values[..., half:], values[..., :half]], axis=-1)
    return values * cosine + turned * sine


def shards(
    tokens,
    gain,
    w_query,
    b_query,
    key_weight,
    b_key,
    value_weight,
    value_bias,
    random_block_index,
    global_block_index,
):
    row_count = lax.axis_size("row")
    here = lax.axis_index("row")
    column = lax.axis_index("col")
    passages, length, _ = tokens.shape
    heads_here = w_query.shape[1] // HEAD_SIZE
    pairs_here = key_weight.shape[1] // HEAD_SIZE
    passage_groups = heads_here // pairs_here
    per_device = length // BLOCK_TOKENS
    scale = 1.0 / math.sqrt(HEAD_SIZE)
    whole = lax.all_gather(tokens, "col", axis=2, tiled=True)
    widened = whole.astype(jnp.float32)
    power = jnp.mean(widened * widened, axis=-1, keepdims=True)
    normed = (
        (widened * lax.rsqrt(power + norm_eps) * gain)
        .astype(jnp.bfloat16)
        .reshape(passages * length, -1)
    )
    token_positions = (here * length + jnp.arange(length, dtype=jnp.int32)).astype(jnp.float32)

    def project(panel):
        return jnp.dot(normed, panel, preferred_element_type=jnp.float32)

    def broadcast_global(own, entry, passage_index, local_head):
        owner = entry // per_device
        offset = entry % per_device
        candidate = lax.dynamic_index_in_dim(
            own[passage_index, :, local_head], offset, 0, keepdims=False
        )
        return broadcast(candidate, "row", owner)

    query_panel, key_panel, value_panel = (
        lax.all_gather(w_query, "row", axis=0, tiled=True),
        lax.all_gather(key_weight, "row", axis=0, tiled=True),
        lax.all_gather(value_weight, "row", axis=0, tiled=True),
    )
    key = apply_rotation(
        (project(key_panel) + b_key).reshape(passages, length, pairs_here, HEAD_SIZE),
        token_positions,
    ).astype(jnp.bfloat16)
    value_rows = (
        (project(value_panel) + value_bias)
        .astype(jnp.bfloat16)
        .reshape(passages, length, pairs_here, HEAD_SIZE)
    )
    pairs = jnp.concatenate([key, value_rows], axis=-1)
    width = pairs_here * 2 * HEAD_SIZE
    padded = padded_2(pairs.reshape(passages, length, width), (("row", 1),), BLOCK_TOKENS)
    padded_blocks = padded.reshape(
        passages, per_device + 2, BLOCK_TOKENS, pairs_here, 2 * HEAD_SIZE
    )
    window = jnp.stack([padded_blocks[:, step : step + per_device] for step in range(3)], axis=2)
    window = window.reshape(passages, per_device, 3 * BLOCK_TOKENS, pairs_here, 2 * HEAD_SIZE)
    own = pairs.reshape(passages, per_device, BLOCK_TOKENS, pairs_here, 2 * HEAD_SIZE).transpose(
        0, 1, 3, 2, 4
    )
    global_here = lax.dynamic_slice_in_dim(global_block_index, column * pairs_here, pairs_here, 1)
    global_pairs = jnp.stack(
        [
            jnp.stack(
                [
                    jnp.stack(
                        [
                            broadcast_global(
                                own, global_here[passage_index, 0, slot], passage_index, 0
                            )
                            for slot in range(GLOBAL_BLOCKS)
                        ]
                    )
                ]
            )
            for passage_index in range(passages)
        ]
    )
    global_pairs = global_pairs.reshape(
        passages, pairs_here, GLOBAL_BLOCKS * BLOCK_TOKENS, 2 * HEAD_SIZE
    )
    selected = lax.dynamic_slice_in_dim(random_block_index, column * heads_here, heads_here, 2)
    rotation_table = selected.reshape(passages, row_count, per_device, heads_here, RANDOM_BLOCKS)
    rotation_table = rotation_table.transpose(1, 0, 2, 3, 4).reshape(row_count, -1)
    owners = rotation_table // per_device
    wanted = rotation_table.shape[1]
    capacity = (wanted + row_count - 1) // row_count
    order = jnp.arange(wanted, dtype=jnp.int32)
    earlier = order[None, :] < order[:, None]
    matches = (owners[:, :, None] == owners[:, None, :]) & earlier[None, :, :]
    rank = jnp.sum(matches, axis=2, dtype=jnp.int32)
    passage_of = order // (per_device * heads_here * RANDOM_BLOCKS)
    head_of = order // RANDOM_BLOCKS % heads_here
    source = (passage_of[None, :] * per_device + rotation_table % per_device) * pairs_here + (
        head_of // passage_groups
    )[None, :]
    slots = jnp.arange(capacity, dtype=jnp.int32)
    chosen = (owners[:, None, :] == here) & (rank[:, None, :] == slots[None, :, None])
    valid = jnp.any(chosen, axis=2)
    pick = jnp.sum(jnp.where(chosen, source[:, None, :], 0), axis=2)
    flat_blocks = own.reshape(-1, BLOCK_TOKENS, 2 * HEAD_SIZE)
    outgoing = jnp.where(valid[:, :, None, None], flat_blocks[pick], jnp.zeros((), jnp.bfloat16))
    incoming = lax.all_to_all(outgoing, "row", split_axis=0, concat_axis=0, tiled=True)
    mine_owner = lax.dynamic_index_in_dim(owners, here, 0, keepdims=False)
    mine_rank = lax.dynamic_index_in_dim(rank, here, 0, keepdims=False)
    arrived = incoming.reshape(row_count * capacity, BLOCK_TOKENS, 2 * HEAD_SIZE)[
        mine_owner * capacity + mine_rank
    ]
    arrived = arrived.reshape(
        passages,
        per_device,
        pairs_here,
        passage_groups,
        RANDOM_BLOCKS * BLOCK_TOKENS,
        2 * HEAD_SIZE,
    )
    window, global_pairs, arrived = (window, global_pairs, arrived)
    shaped = (project(query_panel) + b_query).reshape(passages, length, heads_here, HEAD_SIZE)
    query_rows = apply_rotation(shaped, token_positions).astype(jnp.bfloat16)
    query_block_rows = query_rows.reshape(
        passages, per_device, BLOCK_TOKENS, pairs_here, passage_groups, HEAD_SIZE
    )
    first = jnp.einsum(
        "sqbkgh,sqwkh->sqkgbw",
        query_block_rows,
        window[..., :HEAD_SIZE],
        preferred_element_type=jnp.float32,
    )
    second = jnp.einsum(
        "sqbkgh,skwh->sqkgbw",
        query_block_rows,
        global_pairs[..., :HEAD_SIZE],
        preferred_element_type=jnp.float32,
    )
    third = jnp.einsum(
        "sqbkgh,sqkgwh->sqkgbw",
        query_block_rows,
        arrived[..., :HEAD_SIZE],
        preferred_element_type=jnp.float32,
    )
    scores = jnp.concatenate([first, second, third], axis=-1) * scale
    nearby_blocks = (
        here * per_device
        + jnp.arange(per_device, dtype=jnp.int32)[:, None]
        + jnp.arange(3, dtype=jnp.int32)[None, :]
        - 1
    )
    inside = (nearby_blocks >= 0) & (nearby_blocks < row_count * per_device)
    mask = jnp.concatenate(
        [
            jnp.repeat(inside, BLOCK_TOKENS, axis=1),
            jnp.ones((per_device, (GLOBAL_BLOCKS + RANDOM_BLOCKS) * BLOCK_TOKENS), dtype=jnp.bool_),
        ],
        axis=1,
    )
    scores = jnp.where(mask[None, :, None, None, None, :], scores, -jnp.inf)
    top = jnp.max(scores, axis=-1, keepdims=True)
    weights = jnp.exp(scores - top)
    probs = (weights / jnp.sum(weights, axis=-1, keepdims=True)).astype(jnp.bfloat16)
    near_probs = probs[..., : 3 * BLOCK_TOKENS]
    global_probs = probs[..., 3 * BLOCK_TOKENS : (3 + GLOBAL_BLOCKS) * BLOCK_TOKENS]
    random_probs = probs[..., (3 + GLOBAL_BLOCKS) * BLOCK_TOKENS :]
    mixed = jnp.einsum(
        "sqkgbw,sqwkh->sqbkgh",
        near_probs,
        window[..., HEAD_SIZE:],
        preferred_element_type=jnp.float32,
    )
    mixed = mixed + jnp.einsum(
        "sqkgbw,skwh->sqbkgh",
        global_probs,
        global_pairs[..., HEAD_SIZE:],
        preferred_element_type=jnp.float32,
    )
    mixed = mixed + jnp.einsum(
        "sqkgbw,sqkgwh->sqbkgh",
        random_probs,
        arrived[..., HEAD_SIZE:],
        preferred_element_type=jnp.float32,
    )
    return mixed.reshape(passages, length, heads_here * HEAD_SIZE).astype(jnp.bfloat16)


def solution(mesh):
    placed = (
        P("groups", "row", "col"),
        P(),
        P("row", "col"),
        P("col"),
        P("row", "col"),
        P("col"),
        P("row", "col"),
        P("col"),
        P("groups", None, None, None),
        P("groups", None, None),
    )
    return jax.shard_map(
        shards, mesh=mesh, in_specs=placed, out_specs=P("groups", "row", "col"), check_vma=False
    )
```

profile of v0, /device:TPU:0, one launch (start us, length us, event | category | flops | bytes accessed | tf_op | source)
XLA Modules:
  0.0 309.3 jit_solution(14698062382800990715)
XLA Ops:
  6.5 0.7 all-gather.3.cloned.1.call-update
  7.3 0.0 all-reduce.4.cloned.1.call-start
  7.3 1.4 constant_dynamic-slice_fusion.5
  18.5 0.3 multiply_cosine_fusion.1
  18.8 0.1 pad_maximum_fusion.5
  19.0 36.6 %all_gather.13 = bf16[3584,128]{1,0:T(8,128)(2,1)} all-gather(bf16[448,128]{1,0:T(8,128)(2,1)} %param.14), channel_id=1, replica_groups=mesh['groups'=2,'row'=8,'col'=2] {'row'}, dimensions={0}, use_global_device_ids=true | all-gather | bytes 1032192 | tf_op jit(solution)/shard_map/all_gather | solution.py:87
  55.5 32.6 %all_gather.14 = bf16[3584,128]{1,0:T(8,128)(2,1)S(1)} all-gather(bf16[448,128]{1,0:T(8,128)(2,1)} %param.16), channel_id=1, replica_groups=mesh['groups'=2,'row'=8,'col'=2] {'row'}, dimensions={0}, use_global_device_ids=true | all-gather | bytes 1032192 | tf_op jit(solution)/shard_map/all_gather | solution.py:88
  88.1 2.0 fusion
  90.1 2.0 fusion.2
  92.2 0.6 convolution_add_fusion.2
  92.8 0.1 slice_negate_fusion
  92.9 0.6 fusion.8
  93.6 0.1 fusion.17
  93.7 0.6 dynamic-slice_select_fusion.1
  94.3 0.6 dynamic-slice_select_fusion.3
  95.0 0.0 all-gather.5.cloned.1.call-start
  95.0 0.7 all-gather.5.cloned.1.call-update
  95.8 0.1 copy.100
  95.9 0.1 copy.79
  96.0 0.1 copy.80
  96.1 0.3 convert_reduce_fusion
  96.4 0.2 fusion.29
  96.6 0.1 copy.84
  96.8 0.2 select_reduce_fusion
  97.0 0.1 copy.85
  97.1 0.1 reshape.590
  97.2 0.1 fusion.19
  97.4 2.0 gather_fusion
  99.3 3.0 broadcast_select_fusion
  102.3 5.9 %all-to-all-start = ((bf16[8,7,64,256]{3,2,1,0:T(8,128)(2,1)}), bf16[8,7,64,256]{3,2,1,0:T(8,128)(2,1)}, u32[]{:S(2)}, u32[]{:S(2)}) async-start(bf16[8,7,64,256]{3,2,1,0:T(8,128)(2,1)} %broadcast_select_fusion), calls=%async_computation | async-start | bytes 3670016 | tf_op jit(solution)/shard_map/all_to_all | solution.py:152
  108.2 0.1 compare_and_fusion
  108.2 0.1 broadcast_in_dim.30
  108.3 0.1 reshape.568
  108.5 0.3 multiply_cosine_fusion
  108.8 0.8 pad_maximum_fusion.7
  109.6 3.9 %collective-permute-start = (bf16[2,64,256]{2,1,0:T(8,128)(2,1)S(1)}, bf16[2,64,256]{2,1,0:T(8,128)(2,1)S(1)}, u32[]{:S(2)}, u32[]{:S(2)}) collective-permute-start(bf16[2,64,256]{2,1,0:T(8,128)(2,1)S(1)} %get-tuple-element.16), channel_id=1, source_target_pairs={{0,2},{2,4},{4,6},{6,8},{8,10},{10,12},{12,14},{1,3},{3,5},{5,7},{... | collective-permute-start | bytes 196616 | tf_op jit(solution)/shard_map/ppermute | solution.py:27
  113.5 1.5 collective-permute-start.1
  115.0 0.7 collective-permute-done
  115.7 5.5 %collective-permute-done.1 = bf16[2,64,256]{2,1,0:T(8,128)(2,1)S(1)} collective-permute-done((bf16[2,64,256]{2,1,0:T(8,128)(2,1)S(1)}, bf16[2,64,256]{2,1,0:T(8,128)(2,1)S(1)}, u32[]{:S(2)}, u32[]{:S(2)}) %collective-permute-start.1) | collective-permute-done | bytes 65568 | tf_op jit(solution)/shard_map/ppermute | solution.py:28
  121.2 0.8 pad_maximum_fusion
  122.0 55.7 %all-reduce.4.cloned.1.call-done = (bf16[1,64,256]{2,1,0:T(8,128)(2,1)}, bf16[1,64,256]{2,1,0:T(8,128)(2,1)}, bf16[1,64,256]{2,1,0:T(8,128)(2,1)}, bf16[1,64,256]{2,1,0:T(8,128)(2,1)}) async-done(((bf16[1,64,256]{2,1,0:T(8,128)(2,1)}, bf16[1,64,256]{2,1,0:T(8,128)(2,1)}, bf16[1,64,256]{2,1,0:T(8,128)(2,1)}, bf16[1,64,256]{2,1,0:T(8,128)(2,1)}), (bf16[1,64,256]{2,1,0:T(8,128)(2,1)}, ...) | async-done | bytes 131088 | tf_op jit(solution)/shard_map/psum | solution.py:17
  177.8 0.8 pad_maximum_fusion.9
  178.6 0.8 pad_maximum_fusion.10
  179.3 3.5 %gather_fusion.1 = bf16[56,64,256]{2,1,0:T(8,128)(2,1)} fusion(bf16[56,64,256]{2,1,0:T(8,128)(2,1)} %bitcast.44, s32[1024]{0:T(1024)S(1)} %pad_clamp_fusion), kind=kCustom, calls=%fused_computation.1 | custom fusion | bytes 3670240 | tf_op jit(solution)/shard_map/gather | solution.py:155
  182.8 97.3 %all-gather.5.cloned.1.call-done = bf16[3584,896]{1,0:T(8,128)(2,1)} async-done(((bf16[448,896]{1,0:T(8,128)(2,1)}), bf16[3584,896]{1,0:T(8,128)(2,1)}) %all-gather.5.cloned.1.call-update) | async-done | bytes 6422544 | tf_op jit(solution)/shard_map/all_gather | solution.py:86
  280.2 4.9 %convolution_add_fusion = f32[256,896]{1,0:T(8,128)S(1)} fusion(bf16[256,3584]{1,0:T(8,128)(2,1)S(1)} %bitcast.127, bf16[3584,896]{1,0:T(8,128)(2,1)} %all-gather.5.cloned.1.call-done, f32[896]{0:T(1024)S(1)} %copy-done.7), kind=kOutput, calls=%fused_computation.21 | convolution fusion | flops 1644396544 | bytes 9178624 | tf_op jit(solution)/shard_map/dot_general | solution.py:75
  285.1 0.1 reshape.609
  285.3 1.1 reshape.570
  286.4 1.3 fusion.41
  287.7 0.3 copy.98
  288.0 0.8 neg.7
  288.8 1.5 copy.94
  290.3 2.0 fusion.10
  292.3 0.7 convolution_bitcast_fusion.5
  293.0 0.4 convolution_bitcast_fusion
  293.4 0.3 convolution_bitcast_fusion.2
  293.7 1.5 fusion.11
  295.2 2.4 fusion.4
  297.6 2.4 divide_convert_fusion
  300.0 0.4 convolution_bitcast_fusion.4
  300.4 0.4 convolution_bitcast_fusion.3
  300.8 0.3 fusion.7
  301.2 0.3 copy.87
  301.5 1.3 convert_element_type.71
  (43 shorter events, 0.3 us)
Async XLA Ops:
  6.5 89.2 %copy-start = (s32[2,16,14,2]{1,3,2,0:T(2,128)S(1)}, s32[2,16,14,2]{1,3,2,0:T(2,128)}, u32[]{:S(2)}) copy-start(s32[2,16,14,2]{1,3,2,0:T(2,128)} %param.18) | copy-start | bytes 10756
  6.5 83.6 %copy-start.4 = (f32[3584]{0:T(1024)S(1)}, f32[3584]{0:T(1024)}, u32[]{:S(2)}) copy-start(f32[3584]{0:T(1024)} %param.11) | copy-start | bytes 43012
  6.5 81.5 %all-gather.3.cloned.1.call-start = ((), (), s32[]{:S(2)}) async-start(), calls=%async_computation.1 | async-start | bytes 2752512 | tf_op jit(solution)/shard_map/all_gather | solution.py:64
  7.3 170.5 %all-reduce.4.cloned.1.call-start = ((), (), s32[]{:S(2)}) async-start(), calls=%async_computation.3 | async-start | bytes 262144 | tf_op jit(solution)/shard_map/psum | solution.py:17
  18.9 73.2 %copy-start.6 = (f32[128]{0:T(128)S(1)}, f32[128]{0:T(128)}, u32[]{:S(2)}) copy-start(f32[128]{0:T(128)} %param.15) | copy-start | bytes 1540
  88.1 4.1 %copy-start.2 = (bf16[3584,128]{1,0:T(8,128)(2,1)S(1)}, bf16[3584,128]{1,0:T(8,128)(2,1)}, u32[]{:S(2)}) copy-start(bf16[3584,128]{1,0:T(8,128)(2,1)} %all_gather.13) | copy-start | bytes 2752516
  90.1 2.8 copy-start.5
  95.0 185.2 %all-gather.5.cloned.1.call-start = ((), (), s32[]{:S(2)}) async-start(), calls=%async_computation.2 | async-start | bytes 7225344 | tf_op jit(solution)/shard_map/all_gather | solution.py:86
  102.3 77.1 %all-to-all-start = ((bf16[8,7,64,256]{3,2,1,0:T(8,128)(2,1)}), bf16[8,7,64,256]{3,2,1,0:T(8,128)(2,1)}, u32[]{:S(2)}, u32[]{:S(2)}) async-start(bf16[8,7,64,256]{3,2,1,0:T(8,128)(2,1)} %broadcast_select_fusion), calls=%async_computation | async-start | bytes 3670016 | tf_op jit(solution)/shard_map/all_to_all | solution.py:152
  108.1 172.0 %copy-start.7 = (f32[896]{0:T(1024)S(1)}, f32[896]{0:T(1024)}, u32[]{:S(2)}) copy-start(f32[896]{0:T(1024)} %param.13) | copy-start | bytes 10756
  109.6 6.1 %collective-permute-start = (bf16[2,64,256]{2,1,0:T(8,128)(2,1)S(1)}, bf16[2,64,256]{2,1,0:T(8,128)(2,1)S(1)}, u32[]{:S(2)}, u32[]{:S(2)}) collective-permute-start(bf16[2,64,256]{2,1,0:T(8,128)(2,1)S(1)} %get-tuple-element.16), channel_id=1, source_target_pairs={{0,2},{2,4},{4,6},{6,8},{8,10},{10,12},{12,14},{1,3},{3,5},{5,7},{... | collective-permute-start | bytes 196616 | tf_op jit(solution)/shard_map/ppermute | solution.py:27
  113.5 7.7 %collective-permute-start.1 = (bf16[2,64,256]{2,1,0:T(8,128)(2,1)S(1)}, bf16[2,64,256]{2,1,0:T(8,128)(2,1)S(1)}, u32[]{:S(2)}, u32[]{:S(2)}) collective-permute-start(bf16[2,64,256]{2,1,0:T(8,128)(2,1)S(1)} %get-tuple-element.17), channel_id=1, source_target_pairs={{2,0},{4,2},{6,4},{8,6},{10,8},{12,10},{14,12},{3,1},{5,3},{7,5},{... | collective-permute-start | bytes 196616 | tf_op jit(solution)/shard_map/ppermute | solution.py:28
  287.7 4.6 %copy-start.1 = (bf16[56,64,256]{2,1,0:T(8,128)(2,1)S(1)}, bf16[56,64,256]{2,1,0:T(8,128)(2,1)}, u32[]{:S(2)}) copy-start(bf16[56,64,256]{2,1,0:T(8,128)(2,1)} %gather_fusion.1) | copy-start | bytes 5505028
  288.8 4.2 %copy-start.3 = (bf16[2,2,3,64,1,256]{5,3,2,1,0,4:T(8,128)(2,1)S(1)}, bf16[2,2,3,64,1,256]{5,3,2,1,0,4:T(8,128)(2,1)}, u32[]{:S(2)}) copy-start(bf16[2,2,3,64,1,256]{5,3,2,1,0,4:T(8,128)(2,1)} %pad_maximum_fusion) | copy-start | bytes 1179652
Sparse Core Ops, SparseCore 0:
  8.9 12.8 all-gather.2
  95.1 82.6 all-reduce.3
  180.2 99.9 all-gather.4
where the time goes:
time: 310 us; the launch traced here: 309 us
  waiting for transfers between devices  161 us (52%)
  blocking collectives  69.1 us (22%)
  between operations  23.3 us (8%)
  other arithmetic  22.5 us (7%)
  local copies, waits for them, and re-layouts  13.6 us (4%)
  starting transfers between devices  11.3 us (4%)
  matrix products  8.79 us (3%)
    all_gather x1, waiting for transfers between devices, shards(): lax.all_gather(w_query, 'row', axis=0, tiled=True)  97.3 us
    psum x1, waiting for transfers between devices, broadcast(): return lax.psum(block, axis)  55.7 us
    all_gather x1, blocking collectives, shards(): lax.all_gather(key_weight, 'row', axis=0, tiled=True)  36.6 us
    all_gather x1, blocking collectives, shards(): lax.all_gather(value_weight, 'row', axis=0, tiled=True)  32.6 us
  transfers between devices with their start and end apart: 6, of which 4 were waited for; matrix products, arithmetic and copies ran while one was open for 5% of the time, Pallas kernels for 0%

commit v1 on v0

--- a/solution.py
+++ b/solution.py
@@ -14,7 +14,7 @@
 
 def broadcast(block, axis, source):
     block = jnp.where(lax.axis_index(axis) == source, block, jnp.zeros_like(block))
-    return lax.psum(block, axis)
+    return jnp.sum(lax.all_gather(block, axis), axis=0)
 
 
 def padded_2(shard, sides, width):

time: 310 us -> 321 us (1.035)
  blocking collectives: 69.1 us -> 242 us
  waiting for transfers between devices: 161 us -> 1.42 us
    all_gather x0 -> x4, blocking collectives: none -> 168 us  [broadcast(): return jnp.sum(lax.all_gather(block, axis), axis=0)]
    all_gather x1, waiting for transfers between devices: 97.3 us -> 0.01 us  [shards(): lax.all_gather(w_query, 'row', axis=0, tiled=True)]
    psum x1 -> x0, waiting for transfers between devices: 55.7 us -> none  [broadcast(): return lax.psum(block, axis)]
    ppermute x1, waiting for transfers between devices: 5.49 us -> 0.01 us  [padded_2(): after = lax.ppermute(leading, axis, down)]
  transfers between devices with their start and end apart: 6 -> 5, of which waited for: 4 -> 0; matrix products, arithmetic and copies ran while one was open for 5% -> 6% of each run, Pallas kernels for 0% -> 0%
where the time goes in v1:
time: 321 us; the launch traced here: 320 us
  blocking collectives  242 us (75%)
  between operations  24.2 us (8%)
  other arithmetic  19.9 us (6%)
  local copies, waits for them, and re-layouts  12.9 us (4%)
  starting transfers between devices  10.8 us (3%)
  matrix products  8.79 us (3%)
    all_gather x4, blocking collectives, broadcast(): return jnp.sum(lax.all_gather(block, axis), axis=0)  168 us
    all_gather x1, blocking collectives, shards(): lax.all_gather(key_weight, 'row', axis=0, tiled=True)  38.3 us
    all_gather x1, blocking collectives, shards(): lax.all_gather(value_weight, 'row', axis=0, tiled=True)  35.1 us
  transfers between devices with their start and end apart: 5, of which 0 were waited for; matrix products, arithmetic and copies ran while one was open for 6% of the time, Pallas kernels for 0%

profile of v1, /device:TPU:0, one launch (start us, length us, event | category | flops | bytes accessed | tf_op | source)
XLA Modules:
  0.0 319.9 jit_solution(17991290679114975768)
XLA Ops:
  6.5 0.7 all-gather.3.cloned.1.call-update
  7.3 0.0 all-gather.5.cloned.1.call-start
  7.3 0.7 all-gather.5.cloned.1.call-update
  8.0 0.1 copy.118
  8.1 0.1 copy.97
  8.3 0.1 copy.98
  8.4 0.3 convert_reduce_fusion
  8.7 0.2 fusion.29
  8.9 0.1 copy.102
  9.1 0.2 select_reduce_fusion
  9.3 0.1 copy.103
  9.4 0.1 reshape.574
  9.5 0.3 multiply_cosine_fusion.1
  9.8 0.1 pad_maximum_fusion.5
  9.9 0.0 copy-start.6
  9.9 38.3 %all_gather.29 = bf16[3584,128]{1,0:T(8,128)(2,1)} all-gather(bf16[448,128]{1,0:T(8,128)(2,1)} %param.14), channel_id=1, replica_groups=mesh['groups'=2,'row'=8,'col'=2] {'row'}, dimensions={0}, use_global_device_ids=true | all-gather | bytes 1032192 | tf_op jit(solution)/shard_map/all_gather | solution.py:87
  48.2 35.1 %all_gather.30 = bf16[3584,128]{1,0:T(8,128)(2,1)S(1)} all-gather(bf16[448,128]{1,0:T(8,128)(2,1)} %param.16), channel_id=1, replica_groups=mesh['groups'=2,'row'=8,'col'=2] {'row'}, dimensions={0}, use_global_device_ids=true | all-gather | bytes 1032192 | tf_op jit(solution)/shard_map/all_gather | solution.py:88
  83.4 2.0 fusion
  85.4 0.0 copy-start.5
  85.4 2.0 fusion.2
  87.5 0.6 convolution_add_fusion.2
  88.1 0.1 slice_negate_fusion
  88.3 0.1 fusion.19
  88.4 0.6 fusion.8
  89.0 2.0 gather_fusion
  91.0 3.0 broadcast_select_fusion
  94.0 5.6 %all-to-all-start = ((bf16[8,7,64,256]{3,2,1,0:T(8,128)(2,1)}), bf16[8,7,64,256]{3,2,1,0:T(8,128)(2,1)}, u32[]{:S(2)}, u32[]{:S(2)}) async-start(bf16[8,7,64,256]{3,2,1,0:T(8,128)(2,1)} %broadcast_select_fusion), calls=%async_computation | async-start | bytes 3670016 | tf_op jit(solution)/shard_map/all_to_all | solution.py:152
  99.6 0.7 constant_dynamic-slice_fusion.5
  110.6 0.1 compare_and_fusion
  110.7 0.1 broadcast_in_dim.30
  110.8 0.1 reshape.556
  111.0 0.3 multiply_cosine_fusion
  111.3 0.8 pad_maximum_fusion.7
  112.0 0.1 fusion.17
  112.2 3.9 %collective-permute-start = (bf16[2,64,256]{2,1,0:T(8,128)(2,1)S(1)}, bf16[2,64,256]{2,1,0:T(8,128)(2,1)S(1)}, u32[]{:S(2)}, u32[]{:S(2)}) collective-permute-start(bf16[2,64,256]{2,1,0:T(8,128)(2,1)S(1)} %get-tuple-element.12), channel_id=1, source_target_pairs={{0,2},{2,4},{4,6},{6,8},{8,10},{10,12},{12,14},{1,3},{3,5},{5,7},{... | collective-permute-start | bytes 196616 | tf_op jit(solution)/shard_map/ppermute | solution.py:27
  116.1 1.3 collective-permute-start.1
  117.5 75.7 %all_gather.32 = bf16[8,64,256]{2,1,0:T(8,128)(2,1)S(1)} all-gather(bf16[1,64,256]{2,1,0:T(8,128)(2,1)S(1)} %get-tuple-element.20), channel_id=1, replica_groups=mesh['groups'=2,'row'=8,'col'=2] {'row'}, dimensions={0}, use_global_device_ids=true | all-gather | bytes 294912 | tf_op jit(solution)/shard_map/all_gather | solution.py:17
  193.3 30.9 %all_gather.34 = bf16[8,64,256]{2,1,0:T(8,128)(2,1)S(1)} all-gather(bf16[1,64,256]{2,1,0:T(8,128)(2,1)S(1)} %get-tuple-element.18), channel_id=1, replica_groups=mesh['groups'=2,'row'=8,'col'=2] {'row'}, dimensions={0}, use_global_device_ids=true | all-gather | bytes 294912 | tf_op jit(solution)/shard_map/all_gather | solution.py:17
  224.2 0.0 copy-start.8
  224.2 30.8 %all_gather.33 = bf16[8,64,256]{2,1,0:T(8,128)(2,1)S(1)} all-gather(bf16[1,64,256]{2,1,0:T(8,128)(2,1)S(1)} %get-tuple-element.21), channel_id=1, replica_groups=mesh['groups'=2,'row'=8,'col'=2] {'row'}, dimensions={0}, use_global_device_ids=true | all-gather | bytes 294912 | tf_op jit(solution)/shard_map/all_gather | solution.py:17
  255.1 30.9 %all_gather.35 = bf16[8,64,256]{2,1,0:T(8,128)(2,1)S(1)} all-gather(bf16[1,64,256]{2,1,0:T(8,128)(2,1)S(1)} %get-tuple-element.19), channel_id=1, replica_groups=mesh['groups'=2,'row'=8,'col'=2] {'row'}, dimensions={0}, use_global_device_ids=true | all-gather | bytes 294912 | tf_op jit(solution)/shard_map/all_gather | solution.py:17
  286.1 0.0 collective-permute-done.1
  286.2 0.8 pad_maximum_fusion
  286.9 0.0 all-to-all-done
  286.9 3.5 %gather_fusion.1 = bf16[56,64,256]{2,1,0:T(8,128)(2,1)} fusion(bf16[56,64,256]{2,1,0:T(8,128)(2,1)} %bitcast.48, s32[1024]{0:T(1024)S(1)} %pad_clamp_fusion), kind=kCustom, calls=%fused_computation.1 | custom fusion | bytes 3670240 | tf_op jit(solution)/shard_map/gather | solution.py:155
  290.4 4.9 %convolution_add_fusion = f32[256,896]{1,0:T(8,128)S(1)} fusion(bf16[256,3584]{1,0:T(8,128)(2,1)S(1)} %bitcast.131, bf16[3584,896]{1,0:T(8,128)(2,1)} %all-gather.5.cloned.1.call-done, f32[896]{0:T(1024)S(1)} %copy-done.8), kind=kOutput, calls=%fused_computation.21 | convolution fusion | flops 1644396544 | bytes 9178624 | tf_op jit(solution)/shard_map/dot_general | solution.py:75
  295.4 0.1 reshape.593
  295.5 1.2 reshape.558
  296.7 1.3 fusion.41
  298.0 0.3 copy.116
  298.3 0.8 neg.7
  299.1 1.5 copy.112
  300.6 2.0 fusion.10
  302.6 0.7 convolution_bitcast_fusion.5
  303.3 0.4 convolution_bitcast_fusion
  303.7 0.3 convolution_bitcast_fusion.2
  304.0 1.5 fusion.11
  305.5 2.4 fusion.4
  307.9 2.4 divide_convert_fusion
  310.3 0.4 convolution_bitcast_fusion.4
  310.7 0.4 convolution_bitcast_fusion.3
  311.1 0.3 fusion.7
  311.5 0.3 copy.105
  311.8 1.3 convert_element_type.79
  (50 shorter events, 0.5 us)
Async XLA Ops:
  6.5 1.5 copy-start
  6.5 78.9 %copy-start.4 = (f32[3584]{0:T(1024)S(1)}, f32[3584]{0:T(1024)}, u32[]{:S(2)}) copy-start(f32[3584]{0:T(1024)} %param.11) | copy-start | bytes 43012
  6.5 76.8 %all-gather.3.cloned.1.call-start = ((), (), s32[]{:S(2)}) async-start(), calls=%async_computation.1 | async-start | bytes 2752512 | tf_op jit(solution)/shard_map/all_gather | solution.py:64
  7.3 283.2 %all-gather.5.cloned.1.call-start = ((), (), s32[]{:S(2)}) async-start(), calls=%async_computation.2 | async-start | bytes 7225344 | tf_op jit(solution)/shard_map/all_gather | solution.py:86
  9.9 77.6 %copy-start.6 = (f32[128]{0:T(128)S(1)}, f32[128]{0:T(128)}, u32[]{:S(2)}) copy-start(f32[128]{0:T(128)} %param.15) | copy-start | bytes 1540
  83.4 4.1 %copy-start.2 = (bf16[3584,128]{1,0:T(8,128)(2,1)S(1)}, bf16[3584,128]{1,0:T(8,128)(2,1)}, u32[]{:S(2)}) copy-start(bf16[3584,128]{1,0:T(8,128)(2,1)} %all_gather.29) | copy-start | bytes 2752516
  85.4 3.0 copy-start.5
  91.0 8.6 %copy-start.7 = (s32[2,2,2]{2,1,0:T(2,128)S(1)}, s32[2,2,2]{2,1,0:T(2,128)}, u32[]{:S(2)}) copy-start(s32[2,2,2]{2,1,0:T(2,128)} %param.19) | copy-start | bytes 100
  94.0 192.9 %all-to-all-start = ((bf16[8,7,64,256]{3,2,1,0:T(8,128)(2,1)}), bf16[8,7,64,256]{3,2,1,0:T(8,128)(2,1)}, u32[]{:S(2)}, u32[]{:S(2)}) async-start(bf16[8,7,64,256]{3,2,1,0:T(8,128)(2,1)} %broadcast_select_fusion), calls=%async_computation | async-start | bytes 3670016 | tf_op jit(solution)/shard_map/all_to_all | solution.py:152
  112.2 173.9 %collective-permute-start = (bf16[2,64,256]{2,1,0:T(8,128)(2,1)S(1)}, bf16[2,64,256]{2,1,0:T(8,128)(2,1)S(1)}, u32[]{:S(2)}, u32[]{:S(2)}) collective-permute-start(bf16[2,64,256]{2,1,0:T(8,128)(2,1)S(1)} %get-tuple-element.12), channel_id=1, source_target_pairs={{0,2},{2,4},{4,6},{6,8},{8,10},{10,12},{12,14},{1,3},{3,5},{5,7},{... | collective-permute-start | bytes 196616 | tf_op jit(solution)/shard_map/ppermute | solution.py:27
  116.1 170.0 %collective-permute-start.1 = (bf16[2,64,256]{2,1,0:T(8,128)(2,1)S(1)}, bf16[2,64,256]{2,1,0:T(8,128)(2,1)S(1)}, u32[]{:S(2)}, u32[]{:S(2)}) collective-permute-start(bf16[2,64,256]{2,1,0:T(8,128)(2,1)S(1)} %get-tuple-element.13), channel_id=1, source_target_pairs={{2,0},{4,2},{6,4},{8,6},{10,8},{12,10},{14,12},{3,1},{5,3},{7,5},{... | collective-permute-start | bytes 196616 | tf_op jit(solution)/shard_map/ppermute | solution.py:28
  224.2 66.2 %copy-start.8 = (f32[896]{0:T(1024)S(1)}, f32[896]{0:T(1024)}, u32[]{:S(2)}) copy-start(f32[896]{0:T(1024)} %param.13) | copy-start | bytes 10756
  298.0 4.6 %copy-start.1 = (bf16[56,64,256]{2,1,0:T(8,128)(2,1)S(1)}, bf16[56,64,256]{2,1,0:T(8,128)(2,1)}, u32[]{:S(2)}) copy-start(bf16[56,64,256]{2,1,0:T(8,128)(2,1)} %gather_fusion.1) | copy-start | bytes 5505028
  299.1 4.2 %copy-start.3 = (bf16[2,2,3,64,1,256]{5,3,2,1,0,4:T(8,128)(2,1)S(1)}, bf16[2,2,3,64,1,256]{5,3,2,1,0,4:T(8,128)(2,1)}, u32[]{:S(2)}) copy-start(bf16[2,2,3,64,1,256]{5,3,2,1,0,4:T(8,128)(2,1)} %pad_maximum_fusion) | copy-start | bytes 1179652
Sparse Core Ops, SparseCore 0:
  8.9 12.8 all-gather.2
  24.0 145.8 all-gather.4
